TPU v7x, 256 devices: a whole 4x4x8 slice. The times are simulated.
256 devices in a mesh: seq: 32 (over x, z), head: 8 (over y, core).
Axes of the slice: x: 4, y: 4, z: 8, core: 2. Of those that a mesh axis runs over, the one named last changes fastest.
Arguments:
- queries: bfloat16 [16384, 8192], P('seq', 'head'), may hold values from -48 to 48
- keys: bfloat16 [16384, 1024], P('seq', 'head'), may hold values from -48 to 48
- values: bfloat16 [16384, 1024], P('seq', 'head'), may hold values from -6 to 6
- offsets: int32 [64], P('seq'), may hold values from 0 to 24064, as said below
- query_map: bfloat16 [64, 128, 64], P('head'), may hold values from -0.5 to 0.5
- key_map: bfloat16 [64, 128, 64], P('head'), may hold values from -0.5 to 0.5
- window_logit: float32 [64], P('head'), may hold values from -2 to 6
Outputs:
- attn_rows: bfloat16 [16384, 8192], P(('seq', 'head'))
Inputs may be any that keep to these rules, and one draw needn't show every extreme that they name: offsets[0] = 0, and each span's offset exceeds the one before by 256 or 512.
All inputs are finite; a program needn't handle non-finite values.
Results may differ from a plain program's by a relative error of at most 0.004.
The roundings to bfloat16 on the way count: a program that leaves them out, or rounds other values in their place, can miss the bound.
Values may be sent and summed in bfloat16 or wider, within the bound.
No kernel may reach another device: no remote copies, remote signals or barrier semaphores. Data moves between devices by JAX's collectives and lax.ppermute only.
A program may use at most 128 MiB of HBM per device.

v0:
```python
import math
import jax
import jax.numpy as jnp
from jax import lax
from jax.sharding import PartitionSpec as P

WINDOW = 64
BLOCK = 512
SPAN = 256


def passed_along(value, axis, steps):
    names = axis if isinstance(axis, tuple) else (axis,)
    count = math.prod((lax.axis_size(name) for name in names))
    first, last = (max(0, -steps), min(count, count - steps))
    return lax.ppermute(value, axis, [(source, source + steps) for source in range(first, last)])


def angle_tables(positions, half):
    frequency = [500000.0 ** (-float(order) / half) for order in range(half)]
    coarse = jnp.asarray([4096.0 * value % (2.0 * math.pi) for value in frequency], jnp.float32)
    medium = jnp.asarray([64.0 * value % (2.0 * math.pi) for value in frequency], jnp.float32)
    finest = jnp.asarray(frequency, jnp.float32)
    upper = (positions // 4096).astype(jnp.float32)[:, None] * coarse[None, :]
    middle = (positions // 64 % 64).astype(jnp.float32)[:, None] * medium[None, :]
    lower = (positions % 64).astype(jnp.float32)[:, None] * finest[None, :]
    cos_high = jnp.cos(upper) * jnp.cos(middle) - jnp.sin(upper) * jnp.sin(middle)
    sin_high = jnp.sin(upper) * jnp.cos(middle) + jnp.cos(upper) * jnp.sin(middle)
    cosine = cos_high * jnp.cos(lower) - sin_high * jnp.sin(lower)
    sine = sin_high * jnp.cos(lower) + cos_high * jnp.sin(lower)
    return (cosine, sine)


def rotate(rows, cosine, sine):
    half = rows.shape[-1] // 2
    first = rows[..., :half]
    second = rows[..., half:]
    cos_rows = cosine[:, None, :]
    sin_rows = sine[:, None, :]
    return jnp.concatenate(
        [first * cos_rows - second * sin_rows, second * cos_rows + first * sin_rows], axis=-1
    )


def two_softmax(logits):
    return jnp.concatenate(
        [jax.nn.softmax(logits, axis=-1), jax.nn.softmax(-logits, axis=-1)], axis=-1
    )


def split_parts(full_value):
    high_part = full_value.astype(jnp.bfloat16)
    rest_part = (full_value - high_part.astype(jnp.float32)).astype(jnp.bfloat16)
    return (high_part, rest_part)


def body(queries, keys, values, offsets, query_map, key_map, window_logit):
    tokens = queries.shape[0]
    heads = query_map.shape[0]
    head_dim = query_map.shape[1]
    feat = query_map.shape[2]
    kv_local = keys.shape[1] // head_dim
    group = heads // kv_local
    blocks = tokens // BLOCK
    extent = BLOCK + WINDOW
    positions = (offsets[:, None] + jnp.arange(SPAN, dtype=jnp.int32)[None, :]).reshape(tokens)
    cosine, sine = angle_tables(positions, head_dim // 2)
    rot_k = rotate(
        keys.reshape(tokens, kv_local, head_dim).astype(jnp.float32), cosine, sine
    ).astype(jnp.bfloat16)
    value_rows = values.reshape(tokens, kv_local, head_dim)
    tail_keys, tail_values = passed_along(
        (rot_k[tokens - WINDOW :], value_rows[tokens - WINDOW :]), ("sx", "sz"), 1
    )
    ext_keys = jnp.concatenate([tail_keys, rot_k], axis=0)
    ext_values = jnp.concatenate([tail_values, value_rows], axis=0)
    valid = (
        (jnp.arange(tokens + WINDOW) >= WINDOW)
        | (lax.axis_index("sx") > 0)
        | (lax.axis_index("sz") > 0)
    )
    grouped_map = key_map.reshape(kv_local, group, head_dim, feat)
    key_logits = jnp.einsum(
        "ngd,gkdf->ngkf", ext_keys, grouped_map, preferred_element_type=jnp.float32
    )
    phi_key = jnp.where(valid[:, None, None, None], two_softmax(key_logits), 0.0).astype(
        jnp.bfloat16
    )
    lag_phi = phi_key[:tokens].reshape(blocks, BLOCK, kv_local, group, 2 * feat)
    lag_values = ext_values[:tokens].reshape(blocks, BLOCK, kv_local, head_dim)
    block_states = jnp.einsum(
        "bjgkf,bjgd->bgkfd", lag_phi, lag_values, preferred_element_type=jnp.float32
    )
    block_norms = jnp.sum(lag_phi, axis=1, dtype=jnp.float32)
    total_state = jnp.sum(block_states, axis=0)
    total_norm = jnp.sum(block_norms, axis=0)
    before_state = jnp.concatenate(
        [jnp.zeros_like(block_states), jnp.cumsum(block_states, axis=0)[:-1]], axis=0
    )
    before_norm = jnp.concatenate(
        [jnp.zeros_like(block_norms), jnp.cumsum(block_norms, axis=0)[:-1]], axis=0
    )
    state_shape = total_state.shape
    state_size = total_state.size
    packed = jnp.concatenate([total_state.reshape(-1), total_norm.reshape(-1)])

    def exclusive_scan(value, axis):
        count = lax.axis_size(axis)
        inclusive = value
        exclusive = jnp.zeros_like(value)
        first = None
        steps = 1
        while steps < count:
            received = passed_along(inclusive, axis, steps)
            first = received if first is None else first
            exclusive = exclusive + received
            if 2 * steps < count:
                inclusive = inclusive + received
            steps *= 2
        return (exclusive, first)

    row_total = lax.psum(packed, "sz")
    inner, first_received = exclusive_scan(packed, "sz")
    outer, _ = exclusive_scan(row_total, "sx")
    exclusive = inner + outer
    queries, first_received = lax.optimization_barrier((queries, first_received))
    rot_q = rotate(
        queries.reshape(tokens, heads, head_dim).astype(jnp.float32), cosine, sine
    ).astype(jnp.bfloat16)
    query_logits = jnp.einsum("nhd,hdf->nhf", rot_q, query_map, preferred_element_type=jnp.float32)
    phi_query = (
        two_softmax(query_logits).astype(jnp.bfloat16).reshape(tokens, kv_local, group, 2 * feat)
    )
    prior_state = exclusive[:state_size].reshape(state_shape)
    prior_norm = exclusive[state_size:].reshape(total_norm.shape)
    factor = jax.nn.sigmoid(window_logit).reshape(kv_local, group)
    rot_grouped = rot_q.reshape(tokens, kv_local, group, head_dim)
    row_index = jnp.arange(BLOCK)[:, None]
    col_index = jnp.arange(extent)[None, :]
    window_mask = (col_index > row_index) & (col_index <= row_index + WINDOW)
    linear_mask = col_index <= row_index
    live = valid[None, :]
    scores = jnp.einsum(
        "igkd,jgd->gkij", rot_grouped, ext_keys, preferred_element_type=jnp.float32
    ) / math.sqrt(head_dim)
    near_window = window_mask & live
    peak = jnp.max(jnp.where(near_window, scores, -jnp.inf), axis=-1, keepdims=True)
    weights = jnp.where(near_window, jnp.exp(scores - peak), 0.0)
    window_sum = jnp.sum(weights, axis=-1)
    affinity = jnp.einsum("igkf,jgkf->gkij", phi_query, phi_key, preferred_element_type=jnp.float32)
    affinity = jnp.where(linear_mask & live, affinity, 0.0)
    near_sum = jnp.sum(affinity, axis=-1)
    window_num = jnp.einsum(
        "gkij,jgd->igkd",
        weights.astype(jnp.bfloat16),
        ext_values,
        preferred_element_type=jnp.float32,
    )
    near_num = jnp.einsum(
        "gkij,jgd->igkd",
        affinity.astype(jnp.bfloat16),
        ext_values,
        preferred_element_type=jnp.float32,
    )
    state_now = prior_state + before_state[0]
    norm_now = prior_norm + before_norm[0]
    state_high, state_rest = split_parts(state_now)
    norm_high, norm_rest = split_parts(norm_now)
    far_num = jnp.einsum(
        "igkf,gkfd->igkd", phi_query, state_high, preferred_element_type=jnp.float32
    )
    far_num = far_num + jnp.einsum(
        "igkf,gkfd->igkd", phi_query, state_rest, preferred_element_type=jnp.float32
    )
    far_sum = jnp.einsum("igkf,gkf->igk", phi_query, norm_high, preferred_element_type=jnp.float32)
    far_sum = far_sum + jnp.einsum(
        "igkf,gkf->igk", phi_query, norm_rest, preferred_element_type=jnp.float32
    )
    head_factor = factor[None, :, :, None]
    numerator = head_factor * window_num + (1.0 - head_factor) * (near_num + far_num)
    denominator = factor[None] * jnp.transpose(window_sum, (2, 0, 1)) + (1.0 - factor[None]) * (
        jnp.transpose(near_sum, (2, 0, 1)) + far_sum
    )
    outputs = (numerator / denominator[..., None]).astype(jnp.bfloat16)
    result = outputs.reshape(tokens, heads * head_dim)
    return lax.all_to_all(result, "head", split_axis=0, concat_axis=1, tiled=True)


def solution(mesh):
    seq_count = mesh.shape["seq"]
    inner = math.gcd(seq_count, 8)
    split_mesh = jax.sharding.Mesh(
        mesh.devices.reshape(seq_count // inner, inner, mesh.shape["head"]), ("sx", "sz", "head")
    )
    rows = ("sx", "sz")
    in_specs = (
        P(rows, "head"),
        P(rows, "head"),
        P(rows, "head"),
        P(rows),
        P("head", None, None),
        P("head", None, None),
        P("head"),
    )
    out_specs = P(("sx", "sz", "head"), None)
    return jax.shard_map(
        body, mesh=split_mesh, in_specs=in_specs, out_specs=out_specs, check_vma=False
    )
```

profile of v0, /device:TPU:160, one launch (start us, length us, event | category | flops | bytes accessed | tf_op | source)
XLA Modules:
  0.0 221.4 jit_solution(13633600873984047340)
XLA Ops:
  8.4 2.4 %subtract_convert_fusion.3 = (bf16[512,1,64]{0,2,1:T(8,128)(2,1)S(1)}, bf16[512,1,64]{0,2,1:T(8,128)(2,1)S(1)}) fusion(f32[512,1,128]{0,2,1:T(8,128)S(1)} %bitcast_convert_fusion, f32[64]{0:T(128)} %constant.80.clone, f32[512]{0:T(512)S(1)} %get-tuple-element.27, f32[64]{0:T(128)} %constant.79.clone, f32[512]{0:T(512)S(1)} %get-tuple-element.26, ...), kind=kLoop, calls=%fused_computation.118 | loop fusion | flops 753664 | bytes 400128 | tf_op jit(solution)/shard_map/convert.6
  10.8 2.9 %collective-permute-start.1 = (bf16[64,1,128]{0,2,1:T(8,128)(2,1)S(1)}, bf16[64,1,128]{0,2,1:T(8,128)(2,1)S(1)}, u32[]{:S(2)}, u32[]{:S(2)}) collective-permute-start(bf16[64,1,128]{0,2,1:T(8,128)(2,1)S(1)} %pad_maximum_fusion.13), channel_id=1, source_target_pairs={{0,8},{8,16},{16,24},{24,32},{32,40},{40,48},{48,56},{56,64},{64,7... | collective-permute-start | bytes 49160 | tf_op jit(solution)/shard_map/ppermute | solution.py:16
  14.5 2.9 %collective-permute-start = (bf16[64,1,128]{2,0,1:T(8,128)(2,1)S(1)}, bf16[64,1,128]{2,0,1:T(8,128)(2,1)S(1)}, u32[]{:S(2)}, u32[]{:S(2)}) collective-permute-start(bf16[64,1,128]{2,0,1:T(8,128)(2,1)S(1)} %slice_bitcast_fusion), channel_id=1, source_target_pairs={{0,8},{8,16},{16,24},{24,32},{32,40},{40,48},{48,56},{56,64},{64,7... | collective-permute-start | bytes 49160 | tf_op jit(solution)/shard_map/ppermute | solution.py:16
  17.4 2.9 %fusion.64 = (f32[512,64]{0,1:T(8,128)}, f32[512,64]{0,1:T(8,128)}) fusion(f32[64]{0:T(128)} %constant.80.clone, f32[512]{0:T(512)S(1)} %get-tuple-element.27, f32[64]{0:T(128)} %constant.79.clone, f32[512]{0:T(512)S(1)} %get-tuple-element.26, f32[64]{0:T(128)} %constant.78.clone, f32[512]{0:T(512)S(1)} %get-tuple-element.25), kind=kLoop, calls=%fused_computation.105 | loop fusion | flops 491520 | bytes 269056 | tf_op jit(solution)/shard_map/sub | solution.py:29
  21.6 2.4 %fusion.58 = f32[576,512]{0,1} fusion(bf16[128,512]{0,1:T(8,128)(2,1)} %bitcast.177, bf16[512,1,64]{0,2,1:T(8,128)(2,1)S(1)} %get-tuple-element.22, bf16[512,1,64]{0,2,1:T(8,128)(2,1)S(1)} %get-tuple-element.21, bf16[64,1,128]{0,2,1:T(8,128)(2,1)S(1)} %collective-permute-done.1), kind=kOutput, calls=%fused_computation.99 | convolution fusion | flops 75939840 | bytes 1458176
  24.0 2.3 %copy.39 = f32[576,8,64]{2,1,0:T(8,128)S(1)} copy(f32[576,8,64]{0,2,1:T(8,128)} %bitcast.171) | data formatting | bytes 2359296 | tf_op jit(solution)/shard_map/ngd,gkdf->ngkf/dot_general | solution.py:83
  27.6 3.6 %fusion.25 = (f32[576,8]{1,0:T(8,128)S(1)}, f32[576,8]{1,0:T(8,128)S(1)}) fusion(f32[576,8,64]{2,1,0:T(8,128)S(1)} %copy.39, f32[576,8]{1,0:T(8,128)S(1)} %get-tuple-element.9, f32[576,8]{1,0:T(8,128)S(1)} %get-tuple-element.10), kind=kLoop, calls=%fused_computation.39 | loop fusion | flops 1465344 | bytes 1253376 | tf_op jit(solution)/shard_map/reduce_sum | solution.py:47
  31.2 3.1 %fusion.24 = (bf16[576,1,8,64]{3,2,0,1:T(8,128)(2,1)S(1)}, bf16[576,1,8,64]{3,2,0,1:T(8,128)(2,1)S(1)}) fusion(f32[576,8,64]{2,1,0:T(8,128)S(1)} %copy.39, f32[576,8]{1,0:T(8,128)S(1)} %get-tuple-element.7, f32[576,8]{1,0:T(8,128)S(1)} %get-tuple-element.9, f32[576,8]{1,0:T(8,128)S(1)} %get-tuple-element.8, f32[576,8]{1,0:T(8,128)S(1)} %get-tuple-element.10), kind=kLoop, calls=%fused_computation.38 | loop fusion | flops 2064384 | bytes 2433024 | tf_op jit(solution)/shard_map/div | solution.py:47
  34.3 4.0 %convert_reduce_fusion = (f32[8,128]{1,0:T(8,128)S(1)}, bf16[512,1,8,128]{3,2,0,1:T(8,128)(2,1)S(1)}) fusion(bf16[576,1,8,64]{3,2,0,1:T(8,128)(2,1)S(1)} %get-tuple-element.18, bf16[576,1,8,64]{3,2,0,1:T(8,128)(2,1)S(1)} %get-tuple-element.17, pred[512]{0:T(512)(128)(4,1)S(1)} %slice-done), kind=kLoop, calls=%fused_computation.34 | loop fusion | flops 3668992 | bytes 2232832 | tf_op jit(solution)/shard_map/reduce_sum | solution.py:94
  39.7 2.1 collective-permute-start.2
  42.3 1.7 copy.43
  44.1 1.7 copy.45
  45.8 1.8 fusion.33
  47.6 2.9 %fusion.14 = bf16[576,8,128]{2,1,0:T(8,128)(2,1)} fusion(bf16[576,8,64]{2,1,0:T(8,128)(2,1)S(1)} %bitcast.169, bf16[576,8,64]{2,1,0:T(8,128)(2,1)S(1)} %bitcast.168, pred[576]{0:T(1024)(128)(4,1)S(1)} %copy-done.26), kind=kLoop, calls=%fused_computation.18 | loop fusion | flops 2949120 | bytes 2359872 | tf_op jit(solution)/shard_map/convert_element_type | solution.py:86
  50.5 4.4 %collective-permute-done.2 = f32[132096]{0:T(1024)S(1)} collective-permute-done((f32[132096]{0:T(1024)S(1)}, f32[132096]{0:T(1024)S(1)}, u32[]{:S(2)}, u32[]{:S(2)}) %collective-permute-start.2) | collective-permute-done | bytes 528416 | tf_op jit(solution)/shard_map/ppermute | solution.py:16
  54.9 1.7 copy.41
  56.9 1.9 copy.65
  58.8 1.9 copy.66
  60.8 2.8 %subtract_convert_fusion = (bf16[512,8,64]{2,0,1:T(8,128)(2,1)S(1)}, bf16[512,8,64]{2,0,1:T(8,128)(2,1)S(1)}) fusion(f32[512,8,64]{2,0,1:T(8,128)} %copy.66, f32[512,8,64]{2,0,1:T(8,128)} %copy.65, f32[512,64]{1,0:T(8,128)S(1)} %copy-done.19, f32[512,64]{1,0:T(8,128)S(1)} %copy-done.18), kind=kLoop, calls=%fused_computation.33 | loop fusion | flops 2097152 | bytes 3407872 | tf_op jit(solution)/shard_map/convert.4
  64.5 1.9 fusion.110
  66.4 2.1 fusion.107
  68.4 1.9 collective-permute-start.3
  70.4 3.5 %fusion.2 = (f32[8,512]{1,0:T(8,128)S(1)}, f32[576,512,8]{1,0,2:T(8,128)S(1)}) fusion(pred[512,576]{0,1:T(8,128)(4,1)} %get-tuple-element.29, bf16[512,8,64]{2,0,1:T(8,128)(2,1)S(1)} %get-tuple-element.16, bf16[512,8,64]{2,0,1:T(8,128)(2,1)S(1)} %get-tuple-element.15, bf16[512,1,64]{0,2,1:T(8,128)(2,1)S(1)} %copy-done.16, ...), kind=kOutput, calls=%fused_computation.4 | convolution fusion | flops 613593088 | bytes 10944512 | tf_op jit(solution)/shard_map/igkd,jgd->gkij/dot_general | solution.py:143
  73.9 3.7 %copy-done.1 = f32[576,512,8]{1,0,2:T(8,128)} copy-done((f32[576,512,8]{1,0,2:T(8,128)}, f32[576,512,8]{1,0,2:T(8,128)S(1)}, u32[]{:S(2)}) %copy-start.1) | copy-done | bytes 9437208
  77.6 1.9 fusion.5
  79.5 68.3 %all-reduce.2.cloned.1.call-done = f32[132096]{0:T(1024)} async-done(((f32[132096]{0:T(1024)}), f32[132096]{0:T(1024)}) %all-reduce.2.cloned.1.call-update) | async-done | bytes 528400 | tf_op jit(solution)/shard_map/psum | solution.py:122
  147.9 3.5 %collective-permute-start.5 = (f32[132096]{0:T(1024)}, f32[132096]{0:T(1024)S(1)}, u32[]{:S(2)}, u32[]{:S(2)}) collective-permute-start(f32[132096]{0:T(1024)} %all-reduce.2.cloned.1.call-done), channel_id=1, source_target_pairs={{0,64},{64,128},{128,192},{1,65},{65,129},{129,193},{2,66},{66,130... | collective-permute-start | bytes 1585160 | tf_op jit(solution)/shard_map/ppermute | solution.py:16
  151.4 7.1 %fusion.10 = f32[128,8,512]{2,0,1:T(8,128)} fusion(f32[576,512,8]{1,0,2:T(8,128)} %copy-done.1, f32[8,512]{1,0:T(8,128)S(1)} %get-tuple-element.34, pred[512,576]{0,1:T(8,128)(4,1)S(1)} %copy-done.7, bf16[64,1,128]{2,0,1:T(8,128)(2,1)S(1)} %copy-done.32, bf16[512,1,128]{2,0,1:T(8,128)(2,1)S(1)} %bitcast.182), kind=kOutput, calls=%fused_computation.14 | convolution fusion | flops 613711872 | bytes 11993088 | tf_op jit(solution)/shard_map/gkij,jgd->igkd/dot_general | solution.py:153
  161.4 4.8 %collective-permute-start.6 = (f32[132096]{0:T(1024)S(1)}, f32[132096]{0:T(1024)S(1)}, u32[]{:S(2)}, u32[]{:S(2)}) collective-permute-start(f32[132096]{0:T(1024)S(1)} %add.181), channel_id=1, source_target_pairs={{0,128},{64,192},{1,129},{65,193},{2,130},{66,194},{3,131},{67,195... | collective-permute-start | bytes 1585160 | tf_op jit(solution)/shard_map/ppermute | solution.py:16
  166.6 3.6 %select_reduce_fusion = (f32[8,512]{1,0:T(8,128)S(1)}, bf16[8,512,576]{1,2,0:T(8,128)(2,1)}) fusion(pred[512,576]{0,1:T(8,128)(4,1)S(1)} %copy-done.21, bf16[512,8,64]{0,2,1:T(8,128)(2,1)S(1)} %get-tuple-element.38, bf16[512,8,64]{0,2,1:T(8,128)(2,1)S(1)} %get-tuple-element.39, bf16[576,8,128]{2,1,0:T(8,128)(2,1)S(1)} %copy-done.12), kind=kOutput, calls=%fused_computation.7 | convolution fusion | flops 613150720 | bytes 7258112 | tf_op jit(solution)/shard_map/igkf,jgkf->gkij/dot_general | solution.py:150
  170.3 15.6 %collective-permute-done.4 = f32[132096]{0:T(1024)S(1)} collective-permute-done((f32[132096]{0:T(1024)S(1)}, f32[132096]{0:T(1024)S(1)}, u32[]{:S(2)}, u32[]{:S(2)}) %collective-permute-start.4) | collective-permute-done | bytes 528416 | tf_op jit(solution)/shard_map/ppermute | solution.py:16
  193.4 20.1 %all_to_all.19 = bf16[8,64,1024]{2,1,0:T(8,128)(2,1)S(1)} all-to-all(bf16[8,64,1024]{2,1,0:T(8,128)(2,1)S(1)} %all_to_all.14), channel_id=1, replica_groups=mesh['sx'=4,'sz'=8,'head'=8] {'head'}, dimensions={0} | all-to-all | bytes 2097152 | tf_op jit(solution)/shard_map/all_to_all | solution.py:186
  (111 shorter events, 19.8 us)
Async XLA Ops:
  6.5 57.1 %copy-start = (bf16[8,128,64]{1,2,0:T(8,128)(2,1)S(1)}, bf16[8,128,64]{1,2,0:T(8,128)(2,1)}, u32[]{:S(2)}) copy-start(bf16[8,128,64]{1,2,0:T(8,128)(2,1)} %param.14) | copy-start | bytes 393220
  10.7 13.2 %copy-start.13 = (bf16[512,1,64]{0,2,1:T(8,128)(2,1)}, bf16[512,1,64]{0,2,1:T(8,128)(2,1)S(1)}, u32[]{:S(2)}) copy-start(bf16[512,1,64]{0,2,1:T(8,128)(2,1)S(1)} %get-tuple-element.21) | copy-start | bytes 196612
  10.7 13.2 %copy-start.15 = (bf16[512,1,64]{0,2,1:T(8,128)(2,1)}, bf16[512,1,64]{0,2,1:T(8,128)(2,1)S(1)}, u32[]{:S(2)}) copy-start(bf16[512,1,64]{0,2,1:T(8,128)(2,1)S(1)} %get-tuple-element.22) | copy-start | bytes 196612
  10.8 10.7 %collective-permute-start.1 = (bf16[64,1,128]{0,2,1:T(8,128)(2,1)S(1)}, bf16[64,1,128]{0,2,1:T(8,128)(2,1)S(1)}, u32[]{:S(2)}, u32[]{:S(2)}) collective-permute-start(bf16[64,1,128]{0,2,1:T(8,128)(2,1)S(1)} %pad_maximum_fusion.13), channel_id=1, source_target_pairs={{0,8},{8,16},{16,24},{24,32},{32,40},{40,48},{48,56},{56,64},{64,7... | collective-permute-start | bytes 49160 | tf_op jit(solution)/shard_map/ppermute | solution.py:16
  14.5 23.9 %collective-permute-start = (bf16[64,1,128]{2,0,1:T(8,128)(2,1)S(1)}, bf16[64,1,128]{2,0,1:T(8,128)(2,1)S(1)}, u32[]{:S(2)}, u32[]{:S(2)}) collective-permute-start(bf16[64,1,128]{2,0,1:T(8,128)(2,1)S(1)} %slice_bitcast_fusion), channel_id=1, source_target_pairs={{0,8},{8,16},{16,24},{24,32},{32,40},{40,48},{48,56},{56,64},{64,7... | collective-permute-start | bytes 49160 | tf_op jit(solution)/shard_map/ppermute | solution.py:16
  21.6 4.7 %copy-start.25 = (pred[576]{0:T(1024)(128)(4,1)}, pred[576]{0:T(1024)(128)(4,1)S(1)}, u32[]{:S(2)}) copy-start(pred[576]{0:T(1024)(128)(4,1)S(1)} %fusion.85) | copy-start | bytes 1732
  34.3 4.5 %copy-start.2 = (bf16[576,1,8,64]{3,2,0,1:T(8,128)(2,1)}, bf16[576,1,8,64]{3,2,0,1:T(8,128)(2,1)S(1)}, u32[]{:S(2)}) copy-start(bf16[576,1,8,64]{3,2,0,1:T(8,128)(2,1)S(1)} %get-tuple-element.17) | copy-start | bytes 1769476
  34.3 4.5 %copy-start.4 = (bf16[576,1,8,64]{3,2,0,1:T(8,128)(2,1)}, bf16[576,1,8,64]{3,2,0,1:T(8,128)(2,1)S(1)}, u32[]{:S(2)}) copy-start(bf16[576,1,8,64]{3,2,0,1:T(8,128)(2,1)S(1)} %get-tuple-element.18) | copy-start | bytes 1769476
  34.3 4.0 %copy-start.27 = (bf16[512,128]{1,0:T(8,128)(2,1)S(1)}, bf16[512,128]{1,0:T(8,128)(2,1)}, u32[]{:S(2)}) copy-start(bf16[512,128]{1,0:T(8,128)(2,1)} %param.12) | copy-start | bytes 393220
  38.3 7.5 %copy-start.26 = (pred[576]{0:T(1024)(128)(4,1)S(1)}, pred[576]{0:T(1024)(128)(4,1)}, u32[]{:S(2)}) copy-start(pred[576]{0:T(1024)(128)(4,1)} %copy-done.25) | copy-start | bytes 1732
  38.9 8.8 %copy-start.3 = (bf16[576,1,8,64]{3,2,0,1:T(8,128)(2,1)S(1)}, bf16[576,1,8,64]{3,2,0,1:T(8,128)(2,1)}, u32[]{:S(2)}) copy-start(bf16[576,1,8,64]{3,2,0,1:T(8,128)(2,1)} %copy-done.2) | copy-start | bytes 1769476
  38.9 8.8 %copy-start.5 = (bf16[576,1,8,64]{3,2,0,1:T(8,128)(2,1)S(1)}, bf16[576,1,8,64]{3,2,0,1:T(8,128)(2,1)}, u32[]{:S(2)}) copy-start(bf16[576,1,8,64]{3,2,0,1:T(8,128)(2,1)} %copy-done.4) | copy-start | bytes 1769476
  39.7 10.9 %copy-start.8 = (f32[132096]{0:T(1024)}, f32[132096]{0:T(1024)S(1)}, u32[]{:S(2)}) copy-start(f32[132096]{0:T(1024)S(1)} %pad_maximum_fusion.3) | copy-start | bytes 1585156
  39.7 15.2 %collective-permute-start.2 = (f32[132096]{0:T(1024)S(1)}, f32[132096]{0:T(1024)S(1)}, u32[]{:S(2)}, u32[]{:S(2)}) collective-permute-start(f32[132096]{0:T(1024)S(1)} %pad_maximum_fusion.3), channel_id=1, source_target_pairs={{0,8},{8,16},{16,24},{24,32},{32,40},{40,48},{48,56},{1,9},{9,17},... | collective-permute-start | bytes 1585160 | tf_op jit(solution)/shard_map/ppermute | solution.py:16
  54.9 92.9 %all-reduce.2.cloned.1.call-start = ((), (), s32[]{:S(2)}) async-start(), calls=%async_computation.1 | async-start | bytes 1056768 | tf_op jit(solution)/shard_map/psum | solution.py:122
  64.5 5.9 %copy-start.14 = (bf16[512,1,64]{0,2,1:T(8,128)(2,1)S(1)}, bf16[512,1,64]{0,2,1:T(8,128)(2,1)}, u32[]{:S(2)}) copy-start(bf16[512,1,64]{0,2,1:T(8,128)(2,1)} %copy-done.13) | copy-start | bytes 196612
  64.5 5.9 %copy-start.16 = (bf16[512,1,64]{0,2,1:T(8,128)(2,1)S(1)}, bf16[512,1,64]{0,2,1:T(8,128)(2,1)}, u32[]{:S(2)}) copy-start(bf16[512,1,64]{0,2,1:T(8,128)(2,1)} %copy-done.15) | copy-start | bytes 196612
  64.5 5.9 %copy-start.24 = (bf16[64,1,128]{0,2,1:T(8,128)(2,1)S(1)}, bf16[64,1,128]{0,2,1:T(8,128)(2,1)}, u32[]{:S(2)}) copy-start(bf16[64,1,128]{0,2,1:T(8,128)(2,1)} %copy-done.23) | copy-start | bytes 49156
  68.4 90.1 %collective-permute-start.3 = (f32[132096]{0:T(1024)}, f32[132096]{0:T(1024)}, u32[]{:S(2)}, u32[]{:S(2)}) collective-permute-start(f32[132096]{0:T(1024)} %fusion.107), channel_id=1, source_target_pairs={{0,16},{8,24},{16,32},{24,40},{32,48},{40,56},{1,17},{9,25},{17,33... | collective-permute-start | bytes 1585160 | tf_op jit(solution)/shard_map/ppermute | solution.py:16
  70.4 7.2 %copy-start.6 = (pred[512,576]{0,1:T(8,128)(4,1)S(1)}, pred[512,576]{0,1:T(8,128)(4,1)}, u32[]{:S(2)}) copy-start(pred[512,576]{0,1:T(8,128)(4,1)} %get-tuple-element.29) | copy-start | bytes 884740
  73.9 3.7 %copy-start.1 = (f32[576,512,8]{1,0,2:T(8,128)}, f32[576,512,8]{1,0,2:T(8,128)S(1)}, u32[]{:S(2)}) copy-start(f32[576,512,8]{1,0,2:T(8,128)S(1)} %get-tuple-element.35) | copy-start | bytes 28311556
  77.6 73.8 %copy-start.7 = (pred[512,576]{0,1:T(8,128)(4,1)S(1)}, pred[512,576]{0,1:T(8,128)(4,1)}, u32[]{:S(2)}) copy-start(pred[512,576]{0,1:T(8,128)(4,1)} %get-tuple-element.29) | copy-start | bytes 884740
  77.6 73.8 %copy-start.28 = (bf16[512,128]{1,0:T(8,128)(2,1)S(1)}, bf16[512,128]{1,0:T(8,128)(2,1)}, u32[]{:S(2)}) copy-start(bf16[512,128]{1,0:T(8,128)(2,1)} %param.12) | copy-start | bytes 393220
  77.6 73.9 %copy-start.32 = (bf16[64,1,128]{2,0,1:T(8,128)(2,1)S(1)}, bf16[64,1,128]{2,0,1:T(8,128)(2,1)}, u32[]{:S(2)}) copy-start(bf16[64,1,128]{2,0,1:T(8,128)(2,1)} %copy-done.31) | copy-start | bytes 49156
  147.9 13.5 %copy-start.20 = (f32[132096]{0:T(1024)S(1)}, f32[132096]{0:T(1024)}, u32[]{:S(2)}) copy-start(f32[132096]{0:T(1024)} %all-reduce.2.cloned.1.call-done) | copy-start | bytes 1585156
  147.9 13.5 %collective-permute-start.5 = (f32[132096]{0:T(1024)}, f32[132096]{0:T(1024)S(1)}, u32[]{:S(2)}, u32[]{:S(2)}) collective-permute-start(f32[132096]{0:T(1024)} %all-reduce.2.cloned.1.call-done), channel_id=1, source_target_pairs={{0,64},{64,128},{128,192},{1,65},{65,129},{129,193},{2,66},{66,130... | collective-permute-start | bytes 1585160 | tf_op jit(solution)/shard_map/ppermute | solution.py:16
  158.6 7.7 %copy-start.17 = (f32[512,8,64]{0,2,1:T(8,128)S(1)}, f32[512,8,64]{0,2,1:T(8,128)}, u32[]{:S(2)}) copy-start(f32[512,8,64]{0,2,1:T(8,128)} %get-tuple-element.31) | copy-start | bytes 3145732
  159.9 6.7 %copy-start.12 = (bf16[576,8,128]{2,1,0:T(8,128)(2,1)S(1)}, bf16[576,8,128]{2,1,0:T(8,128)(2,1)}, u32[]{:S(2)}) copy-start(bf16[576,8,128]{2,1,0:T(8,128)(2,1)} %fusion.14) | copy-start | bytes 3538948
  159.9 6.7 %copy-start.21 = (pred[512,576]{0,1:T(8,128)(4,1)S(1)}, pred[512,576]{0,1:T(8,128)(4,1)}, u32[]{:S(2)}) copy-start(pred[512,576]{0,1:T(8,128)(4,1)} %get-tuple-element.28) | copy-start | bytes 884740
  159.9 26.0 %collective-permute-start.4 = (f32[132096]{0:T(1024)S(1)}, f32[132096]{0:T(1024)S(1)}, u32[]{:S(2)}, u32[]{:S(2)}) collective-permute-start(f32[132096]{0:T(1024)S(1)} %add.179), channel_id=1, source_target_pairs={{0,32},{8,40},{16,48},{24,56},{1,33},{9,41},{17,49},{25,57},{2,34}... | collective-permute-start | bytes 1585160 | tf_op jit(solution)/shard_map/ppermute | solution.py:16
  161.4 24.5 %collective-permute-start.6 = (f32[132096]{0:T(1024)S(1)}, f32[132096]{0:T(1024)S(1)}, u32[]{:S(2)}, u32[]{:S(2)}) collective-permute-start(f32[132096]{0:T(1024)S(1)} %add.181), channel_id=1, source_target_pairs={{0,128},{64,192},{1,129},{65,193},{2,130},{66,194},{3,131},{67,195... | collective-permute-start | bytes 1585160 | tf_op jit(solution)/shard_map/ppermute | solution.py:16
  166.6 19.3 %copy-start.10 = (f32[132096]{0:T(1024)S(1)}, f32[132096]{0:T(1024)}, u32[]{:S(2)}) copy-start(f32[132096]{0:T(1024)} %copy-done.9) | copy-start | bytes 1585156
  (12 other events, 21.1 us)
Sparse Core Ops, SparseCore 0:
  66.5 81.3 all-reduce.1
where the time goes:
time: 222 us; the launch traced here: 221 us
  waiting for transfers between devices  88.4 us (40%)
  other arithmetic  34.5 us (16%)
  matrix products  22.5 us (10%)
  local copies, waits for them, and re-layouts  22.3 us (10%)
  blocking collectives  20.1 us (9%)
  starting transfers between devices  19.6 us (9%)
  between operations  14 us (6%)
    psum x1, waiting for transfers between devices, body(): row_total = lax.psum(packed, 'sz')  68.3 us
    all_to_all x1, blocking collectives, body(): lax.all_to_all(result, 'head', split_axis=0, concat_axis=1, tiled=True)  20.1 us
    ppermute x7, waiting for transfers between devices, passed_along(): lax.ppermute(value, axis, [(source, source + steps) for source in range(f...  20 us
    ppermute x7, starting transfers between devices, passed_along(): lax.ppermute(value, axis, [(source, source + steps) for source in range(f...  19.6 us
    unnamed x74, local copies, waits for them, and re-layouts  11.3 us
    dot_general x1, matrix products, body(): jnp.einsum('gkij,jgd->igkd', weights.astype(jnp.bfloat16), ext_values, pr...  7.13 us
    another operation x3, other arithmetic  5.46 us
  transfers between devices with their start and end apart: 8, of which 3 were waited for; matrix products, arithmetic and copies ran while one was open for 23% of the time, Pallas kernels for 0%

commit v1 on v0

--- a/solution.py
+++ b/solution.py
@@ -119,7 +119,7 @@
             steps *= 2
         return (exclusive, first)
 
-    row_total = lax.psum(packed, "sz")
+    row_total = jnp.sum(lax.all_gather(packed, "sz"), axis=0)
     inner, first_received = exclusive_scan(packed, "sz")
     outer, _ = exclusive_scan(row_total, "sx")
     exclusive = inner + outer

time: 222 us -> 207 us (0.932)
  waiting for transfers between devices: 88.4 us -> 63.4 us
  local copies, waits for them, and re-layouts: 22.3 us -> 26.2 us
  other arithmetic: 34.5 us -> 38 us
    psum x1 -> x0, waiting for transfers between devices: 68.3 us -> none  [body(): row_total = lax.psum(packed, 'sz')]
    all_gather x0 -> x1, waiting for transfers between devices: none -> 34.8 us  [body(): row_total = jnp.sum(lax.all_gather(packed, 'sz'), axis=0)]
    ppermute x7, waiting for transfers between devices: 20 us -> 28.6 us  [passed_along(): lax.ppermute(value, axis, [(source, source + steps) for source in range(f...]
    reduce_sum x0 -> x1, other arithmetic: none -> 7.07 us  [body(): row_total = jnp.sum(lax.all_gather(packed, 'sz'), axis=0)]
    all_gather x0 -> x1, local copies, waits for them, and re-layouts: none -> 4.77 us  [body(): row_total = jnp.sum(lax.all_gather(packed, 'sz'), axis=0)]
    unnamed x74 -> x64, local copies, waits for them, and re-layouts: 11.3 us -> 11.3 us
  transfers between devices with their start and end apart: 8 -> 8, of which waited for: 3 -> 4; matrix products, arithmetic and copies ran while one was open for 23% -> 33% of each run, Pallas kernels for 0% -> 0%
where the time goes in v1:
time: 207 us; the launch traced here: 205 us
  waiting for transfers between devices  63.4 us (31%)
  other arithmetic  38 us (18%)
  local copies, waits for them, and re-layouts  26.2 us (13%)
  matrix products  22.6 us (11%)
  starting transfers between devices  21 us (10%)
  blocking collectives  20.2 us (10%)
  between operations  14 us (7%)
    all_gather x1, waiting for transfers between devices, body(): row_total = jnp.sum(lax.all_gather(packed, 'sz'), axis=0)  34.8 us
    ppermute x7, waiting for transfers between devices, passed_along(): lax.ppermute(value, axis, [(source, source + steps) for source in range(f...  28.6 us
    ppermute x7, starting transfers between devices, passed_along(): lax.ppermute(value, axis, [(source, source + steps) for source in range(f...  21 us
    all_to_all x1, blocking collectives, body(): lax.all_to_all(result, 'head', split_axis=0, concat_axis=1, tiled=True)  20.2 us
    unnamed x64, local copies, waits for them, and re-layouts  11.3 us
    dot_general x1, matrix products, body(): jnp.einsum('gkij,jgd->igkd', weights.astype(jnp.bfloat16), ext_values, pr...  7.13 us
    reduce_sum x1, other arithmetic, body(): row_total = jnp.sum(lax.all_gather(packed, 'sz'), axis=0)  7.07 us
    another operation x3, other arithmetic  5.49 us
  transfers between devices with their start and end apart: 8, of which 4 were waited for; matrix products, arithmetic and copies ran while one was open for 33% of the time, Pallas kernels for 0%

profile of v1, /device:TPU:160, one launch (start us, length us, event | category | flops | bytes accessed | tf_op | source)
XLA Modules:
  0.0 205.4 jit_solution(12764744628151235673)
XLA Ops:
  8.4 2.4 %subtract_convert_fusion.3 = (bf16[512,1,64]{0,2,1:T(8,128)(2,1)S(1)}, bf16[512,1,64]{0,2,1:T(8,128)(2,1)S(1)}) fusion(f32[512,1,128]{0,2,1:T(8,128)S(1)} %bitcast_convert_fusion, f32[64]{0:T(128)} %constant.80.clone, f32[512]{0:T(512)S(1)} %get-tuple-element.27, f32[64]{0:T(128)} %constant.79.clone, f32[512]{0:T(512)S(1)} %get-tuple-element.26, ...), kind=kLoop, calls=%fused_computation.118 | loop fusion | flops 753664 | bytes 400128 | tf_op jit(solution)/shard_map/convert.6
  10.8 2.9 %collective-permute-start.1 = (bf16[64,1,128]{0,2,1:T(8,128)(2,1)S(1)}, bf16[64,1,128]{0,2,1:T(8,128)(2,1)S(1)}, u32[]{:S(2)}, u32[]{:S(2)}) collective-permute-start(bf16[64,1,128]{0,2,1:T(8,128)(2,1)S(1)} %pad_maximum_fusion.13), channel_id=1, source_target_pairs={{0,8},{8,16},{16,24},{24,32},{32,40},{40,48},{48,56},{56,64},{64,7... | collective-permute-start | bytes 49160 | tf_op jit(solution)/shard_map/ppermute | solution.py:16
  14.5 2.9 %collective-permute-start = (bf16[64,1,128]{2,0,1:T(8,128)(2,1)S(1)}, bf16[64,1,128]{2,0,1:T(8,128)(2,1)S(1)}, u32[]{:S(2)}, u32[]{:S(2)}) collective-permute-start(bf16[64,1,128]{2,0,1:T(8,128)(2,1)S(1)} %slice_bitcast_fusion), channel_id=1, source_target_pairs={{0,8},{8,16},{16,24},{24,32},{32,40},{40,48},{48,56},{56,64},{64,7... | collective-permute-start | bytes 49160 | tf_op jit(solution)/shard_map/ppermute | solution.py:16
  17.4 2.4 %fusion.58 = f32[576,512]{0,1} fusion(bf16[128,512]{0,1:T(8,128)(2,1)} %bitcast.177, bf16[512,1,64]{0,2,1:T(8,128)(2,1)S(1)} %get-tuple-element.22, bf16[512,1,64]{0,2,1:T(8,128)(2,1)S(1)} %get-tuple-element.21, bf16[64,1,128]{0,2,1:T(8,128)(2,1)S(1)} %collective-permute-done.1), kind=kOutput, calls=%fused_computation.99 | convolution fusion | flops 75939840 | bytes 1458176
  19.8 2.3 %copy.61 = f32[576,8,64]{2,1,0:T(8,128)S(1)} copy(f32[576,8,64]{0,2,1:T(8,128)} %bitcast.171) | data formatting | bytes 2359296 | tf_op jit(solution)/shard_map/ngd,gkdf->ngkf/dot_general | solution.py:83
  23.4 3.6 %fusion.25 = (f32[576,8]{1,0:T(8,128)S(1)}, f32[576,8]{1,0:T(8,128)S(1)}) fusion(f32[576,8,64]{2,1,0:T(8,128)S(1)} %copy.61, f32[576,8]{1,0:T(8,128)S(1)} %get-tuple-element.9, f32[576,8]{1,0:T(8,128)S(1)} %get-tuple-element.10), kind=kLoop, calls=%fused_computation.39 | loop fusion | flops 1465344 | bytes 1253376 | tf_op jit(solution)/shard_map/reduce_sum | solution.py:47
  27.0 3.1 %fusion.24 = (bf16[576,1,8,64]{3,2,0,1:T(8,128)(2,1)S(1)}, bf16[576,1,8,64]{3,2,0,1:T(8,128)(2,1)S(1)}) fusion(f32[576,8,64]{2,1,0:T(8,128)S(1)} %copy.61, f32[576,8]{1,0:T(8,128)S(1)} %get-tuple-element.7, f32[576,8]{1,0:T(8,128)S(1)} %get-tuple-element.9, f32[576,8]{1,0:T(8,128)S(1)} %get-tuple-element.8, f32[576,8]{1,0:T(8,128)S(1)} %get-tuple-element.10), kind=kLoop, calls=%fused_computation.38 | loop fusion | flops 2064384 | bytes 2433024 | tf_op jit(solution)/shard_map/div | solution.py:47
  30.2 4.0 %convert_reduce_fusion = (f32[8,128]{1,0:T(8,128)S(1)}, bf16[512,1,8,128]{3,2,0,1:T(8,128)(2,1)S(1)}) fusion(bf16[576,1,8,64]{3,2,0,1:T(8,128)(2,1)S(1)} %get-tuple-element.18, bf16[576,1,8,64]{3,2,0,1:T(8,128)(2,1)S(1)} %get-tuple-element.17, pred[512]{0:T(512)(128)(4,1)S(1)} %slice-done), kind=kLoop, calls=%fused_computation.34 | loop fusion | flops 3668992 | bytes 2232832 | tf_op jit(solution)/shard_map/reduce_sum | solution.py:94
  36.5 2.2 %fusion.64 = (f32[512,64]{0,1:T(8,128)}, f32[512,64]{0,1:T(8,128)S(1)}) fusion(f32[64]{0:T(128)S(1)} %copy-done.26, f32[512]{0:T(512)S(1)} %get-tuple-element.27, f32[64]{0:T(128)S(1)} %copy-done.25, f32[512]{0:T(512)S(1)} %get-tuple-element.26, f32[64]{0:T(128)S(1)} %copy-done.24, f32[512]{0:T(512)S(1)} %get-tuple-element.25), kind=kLoop, calls=%fused_computation.105 | loop fusion | flops 491520 | bytes 269056 | tf_op jit(solution)/shard_map/sub | solution.py:29
  38.7 2.1 %collective-permute-start.2 = (f32[132096]{0:T(1024)}, f32[132096]{0:T(1024)S(1)}, u32[]{:S(2)}, u32[]{:S(2)}) collective-permute-start(f32[132096]{0:T(1024)} %pad_maximum_fusion.3), channel_id=1, source_target_pairs={{0,8},{8,16},{16,24},{24,32},{32,40},{40,48},{48,56},{1,9},{9,17},... | collective-permute-start | bytes 1585160 | tf_op jit(solution)/shard_map/ppermute | solution.py:16
  40.8 1.7 copy.65
  44.5 2.9 %fusion.14 = bf16[576,8,128]{2,1,0:T(8,128)(2,1)} fusion(bf16[576,8,64]{2,1,0:T(8,128)(2,1)S(1)} %bitcast.169, bf16[576,8,64]{2,1,0:T(8,128)(2,1)S(1)} %bitcast.168, pred[576]{0:T(1024)(128)(4,1)S(1)} %copy-done.21), kind=kLoop, calls=%fused_computation.18 | loop fusion | flops 2949120 | bytes 2359872 | tf_op jit(solution)/shard_map/convert_element_type | solution.py:86
  47.4 11.2 %collective-permute-done.2 = f32[132096]{0:T(1024)S(1)} collective-permute-done((f32[132096]{0:T(1024)}, f32[132096]{0:T(1024)S(1)}, u32[]{:S(2)}, u32[]{:S(2)}) %collective-permute-start.2) | collective-permute-done | bytes 528416 | tf_op jit(solution)/shard_map/ppermute | solution.py:16
  58.6 1.7 copy.63
  60.6 1.9 copy.87
  62.5 2.0 copy.88
  65.3 2.1 %collective-permute-start.3 = (f32[132096]{0:T(1024)}, f32[132096]{0:T(1024)}, u32[]{:S(2)}, u32[]{:S(2)}) collective-permute-start(f32[132096]{0:T(1024)} %fusion.107), channel_id=1, source_target_pairs={{0,16},{8,24},{16,32},{24,40},{32,48},{40,56},{1,17},{9,25},{17,33... | collective-permute-start | bytes 1585160 | tf_op jit(solution)/shard_map/ppermute | solution.py:16
  67.4 2.8 %subtract_convert_fusion = (bf16[512,8,64]{2,0,1:T(8,128)(2,1)S(1)}, bf16[512,8,64]{2,0,1:T(8,128)(2,1)S(1)}) fusion(f32[512,8,64]{2,0,1:T(8,128)} %copy.88, f32[512,8,64]{2,0,1:T(8,128)} %copy.87, f32[512,64]{1,0:T(8,128)S(1)} %copy-done.17, f32[512,64]{1,0:T(8,128)S(1)} %copy-done.16), kind=kLoop, calls=%fused_computation.33 | loop fusion | flops 2097152 | bytes 3407872 | tf_op jit(solution)/shard_map/convert.4
  71.1 1.9 fusion.110
  73.0 3.5 %fusion.2 = (f32[8,512]{1,0:T(8,128)S(1)}, f32[576,512,8]{1,0,2:T(8,128)S(1)}) fusion(pred[512,576]{0,1:T(8,128)(4,1)} %get-tuple-element.29, bf16[512,8,64]{2,0,1:T(8,128)(2,1)S(1)} %get-tuple-element.16, bf16[512,8,64]{2,0,1:T(8,128)(2,1)S(1)} %get-tuple-element.15, bf16[512,1,64]{0,2,1:T(8,128)(2,1)S(1)} %get-tuple-element.22, ...), kind=kOutput, calls=%fused_computation.4 | convolution fusion | flops 613593088 | bytes 10944512 | tf_op jit(solution)/shard_map/igkd,jgd->gkij/dot_general | solution.py:143
  76.5 3.6 %copy-done.2 = f32[576,512,8]{1,0,2:T(8,128)} copy-done((f32[576,512,8]{1,0,2:T(8,128)}, f32[576,512,8]{1,0,2:T(8,128)S(1)}, u32[]{:S(2)}) %copy-start.2) | copy-done | bytes 9437208
  80.1 1.9 fusion.5
  82.1 34.8 %all-gather.3.cloned.1.call-done = f32[1056768]{0:T(1024)} async-done(((f32[132096]{0:T(1024)}), f32[1056768]{0:T(1024)}) %all-gather.3.cloned.1.call-update) | async-done | bytes 4227088 | tf_op jit(solution)/shard_map/all_gather | solution.py:122
  116.8 4.8 %reshape.676 = f32[8,132096]{1,0:T(8,128)} reshape(f32[1056768]{0:T(1024)} %all-gather.3.cloned.1.call-done) | data formatting | bytes 8454144 | tf_op jit(solution)/shard_map/all_gather | solution.py:122
  121.6 7.1 %reduce_sum.87 = f32[132096]{0:T(1024)S(1)} reduce(f32[8,132096]{1,0:T(8,128)} %reshape.676, f32[]{:T(128)} %constant.76.clone.1), dimensions={0}, to_apply=%region_10.11 | reduce | flops 924672 | bytes 4755460 | tf_op jit(solution)/shard_map/reduce_sum | solution.py:122
  128.7 3.4 %collective-permute-start.5 = (f32[132096]{0:T(1024)S(1)}, f32[132096]{0:T(1024)S(1)}, u32[]{:S(2)}, u32[]{:S(2)}) collective-permute-start(f32[132096]{0:T(1024)S(1)} %reduce_sum.87), channel_id=1, source_target_pairs={{0,64},{64,128},{128,192},{1,65},{65,129},{129,193},{2,66},{66,130... | collective-permute-start | bytes 1585160 | tf_op jit(solution)/shard_map/ppermute | solution.py:16
  132.2 7.1 %fusion.10 = f32[128,8,512]{2,0,1:T(8,128)} fusion(f32[576,512,8]{1,0,2:T(8,128)} %copy-done.2, f32[8,512]{1,0:T(8,128)S(1)} %get-tuple-element.34, pred[512,576]{0,1:T(8,128)(4,1)S(1)} %copy-done.8, bf16[64,1,128]{2,0,1:T(8,128)(2,1)S(1)} %collective-permute-done, bf16[512,1,128]{2,0,1:T(8,128)(2,1)S(1)} %bitcast.182), kind=kOutput, calls=%fused_computation.14 | convolution fusion | flops 613711872 | bytes 11993088 | tf_op jit(solution)/shard_map/gkij,jgd->igkd/dot_general | solution.py:153
  140.7 1.6 collective-permute-start.4
  143.5 6.0 %collective-permute-start.6 = (f32[132096]{0:T(1024)S(1)}, f32[132096]{0:T(1024)S(1)}, u32[]{:S(2)}, u32[]{:S(2)}) collective-permute-start(f32[132096]{0:T(1024)S(1)} %add.179), channel_id=1, source_target_pairs={{0,128},{64,192},{1,129},{65,193},{2,130},{66,194},{3,131},{67,195... | collective-permute-start | bytes 1585160 | tf_op jit(solution)/shard_map/ppermute | solution.py:16
  149.8 3.6 %select_reduce_fusion = (f32[8,512]{1,0:T(8,128)S(1)}, bf16[8,512,576]{1,2,0:T(8,128)(2,1)}) fusion(pred[512,576]{0,1:T(8,128)(4,1)S(1)} %copy-done.18, bf16[512,8,64]{0,2,1:T(8,128)(2,1)S(1)} %get-tuple-element.38, bf16[512,8,64]{0,2,1:T(8,128)(2,1)S(1)} %get-tuple-element.39, bf16[576,8,128]{2,1,0:T(8,128)(2,1)S(1)} %copy-done.14), kind=kOutput, calls=%fused_computation.7 | convolution fusion | flops 613150720 | bytes 7258112 | tf_op jit(solution)/shard_map/igkf,jgkf->gkij/dot_general | solution.py:150
  153.5 16.2 %collective-permute-done.4 = f32[132096]{0:T(1024)S(1)} collective-permute-done((f32[132096]{0:T(1024)S(1)}, f32[132096]{0:T(1024)S(1)}, u32[]{:S(2)}, u32[]{:S(2)}) %collective-permute-start.4) | collective-permute-done | bytes 528416 | tf_op jit(solution)/shard_map/ppermute | solution.py:16
  177.2 20.2 %all_to_all.19 = bf16[8,64,1024]{2,1,0:T(8,128)(2,1)S(1)} all-to-all(bf16[8,64,1024]{2,1,0:T(8,128)(2,1)S(1)} %all_to_all.14), channel_id=1, replica_groups=mesh['sx'=4,'sz'=8,'head'=8] {'head'}, dimensions={0} | all-to-all | bytes 2097152 | tf_op jit(solution)/shard_map/all_to_all | solution.py:186
  (103 shorter events, 21.5 us)
Async XLA Ops:
  6.5 63.7 %copy-start = (bf16[8,128,64]{1,2,0:T(8,128)(2,1)S(1)}, bf16[8,128,64]{1,2,0:T(8,128)(2,1)}, u32[]{:S(2)}) copy-start(bf16[8,128,64]{1,2,0:T(8,128)(2,1)} %param.14) | copy-start | bytes 393220
  6.5 110.3 %all-gather.3.cloned.1.call-start = ((), (), s32[]{:S(2)}) async-start(), calls=%async_computation.1 | async-start | bytes 4755456 | tf_op jit(solution)/shard_map/all_gather | solution.py:122
  10.8 6.6 %collective-permute-start.1 = (bf16[64,1,128]{0,2,1:T(8,128)(2,1)S(1)}, bf16[64,1,128]{0,2,1:T(8,128)(2,1)S(1)}, u32[]{:S(2)}, u32[]{:S(2)}) collective-permute-start(bf16[64,1,128]{0,2,1:T(8,128)(2,1)S(1)} %pad_maximum_fusion.13), channel_id=1, source_target_pairs={{0,8},{8,16},{16,24},{24,32},{32,40},{40,48},{48,56},{56,64},{64,7... | collective-permute-start | bytes 49160 | tf_op jit(solution)/shard_map/ppermute | solution.py:16
  14.5 19.8 %collective-permute-start = (bf16[64,1,128]{2,0,1:T(8,128)(2,1)S(1)}, bf16[64,1,128]{2,0,1:T(8,128)(2,1)S(1)}, u32[]{:S(2)}, u32[]{:S(2)}) collective-permute-start(bf16[64,1,128]{2,0,1:T(8,128)(2,1)S(1)} %slice_bitcast_fusion), channel_id=1, source_target_pairs={{0,8},{8,16},{16,24},{24,32},{32,40},{40,48},{48,56},{56,64},{64,7... | collective-permute-start | bytes 49160 | tf_op jit(solution)/shard_map/ppermute | solution.py:16
  17.4 4.7 %copy-start.20 = (pred[576]{0:T(1024)(128)(4,1)}, pred[576]{0:T(1024)(128)(4,1)S(1)}, u32[]{:S(2)}) copy-start(pred[576]{0:T(1024)(128)(4,1)S(1)} %fusion.85) | copy-start | bytes 1732
  27.0 3.2 %slice-start = ((pred[576]{0:T(1024)(128)(4,1)}), pred[512]{0:T(512)(128)(4,1)S(1)}, s32[]{:S(2)}) async-start(pred[576]{0:T(1024)(128)(4,1)} %copy-done.20), calls=%async_computation.2 | async-start | bytes 1024 | tf_op jit(solution)/shard_map/slice | solution.py:89
  30.2 4.6 %copy-start.3 = (bf16[576,1,8,64]{3,2,0,1:T(8,128)(2,1)}, bf16[576,1,8,64]{3,2,0,1:T(8,128)(2,1)S(1)}, u32[]{:S(2)}) copy-start(bf16[576,1,8,64]{3,2,0,1:T(8,128)(2,1)S(1)} %get-tuple-element.17) | copy-start | bytes 1769476
  30.2 4.6 %copy-start.5 = (bf16[576,1,8,64]{3,2,0,1:T(8,128)(2,1)}, bf16[576,1,8,64]{3,2,0,1:T(8,128)(2,1)S(1)}, u32[]{:S(2)}) copy-start(bf16[576,1,8,64]{3,2,0,1:T(8,128)(2,1)S(1)} %get-tuple-element.18) | copy-start | bytes 1769476
  30.2 4.1 %copy-start.22 = (bf16[512,128]{1,0:T(8,128)(2,1)S(1)}, bf16[512,128]{1,0:T(8,128)(2,1)}, u32[]{:S(2)}) copy-start(bf16[512,128]{1,0:T(8,128)(2,1)} %param.12) | copy-start | bytes 393220
  34.2 2.3 %copy-start.24 = (f32[64]{0:T(128)S(1)}, f32[64]{0:T(128)}, u32[]{:S(2)}) copy-start(f32[64]{0:T(128)} %constant.78.clone) | copy-start | bytes 772
  34.2 2.3 %copy-start.25 = (f32[64]{0:T(128)S(1)}, f32[64]{0:T(128)}, u32[]{:S(2)}) copy-start(f32[64]{0:T(128)} %constant.79.clone) | copy-start | bytes 772
  34.2 9.1 %copy-start.21 = (pred[576]{0:T(1024)(128)(4,1)S(1)}, pred[576]{0:T(1024)(128)(4,1)}, u32[]{:S(2)}) copy-start(pred[576]{0:T(1024)(128)(4,1)} %copy-done.20) | copy-start | bytes 1732
  34.8 9.7 %copy-start.4 = (bf16[576,1,8,64]{3,2,0,1:T(8,128)(2,1)S(1)}, bf16[576,1,8,64]{3,2,0,1:T(8,128)(2,1)}, u32[]{:S(2)}) copy-start(bf16[576,1,8,64]{3,2,0,1:T(8,128)(2,1)} %copy-done.3) | copy-start | bytes 1769476
  34.8 9.7 %copy-start.6 = (bf16[576,1,8,64]{3,2,0,1:T(8,128)(2,1)S(1)}, bf16[576,1,8,64]{3,2,0,1:T(8,128)(2,1)}, u32[]{:S(2)}) copy-start(bf16[576,1,8,64]{3,2,0,1:T(8,128)(2,1)} %copy-done.5) | copy-start | bytes 1769476
  38.7 19.9 %collective-permute-start.2 = (f32[132096]{0:T(1024)}, f32[132096]{0:T(1024)S(1)}, u32[]{:S(2)}, u32[]{:S(2)}) collective-permute-start(f32[132096]{0:T(1024)} %pad_maximum_fusion.3), channel_id=1, source_target_pairs={{0,8},{8,16},{16,24},{24,32},{32,40},{40,48},{48,56},{1,9},{9,17},... | collective-permute-start | bytes 1585160 | tf_op jit(solution)/shard_map/ppermute | solution.py:16
  62.5 4.9 %copy-start.16 = (f32[512,64]{1,0:T(8,128)S(1)}, f32[512,64]{1,0:T(8,128)}, u32[]{:S(2)}) copy-start(f32[512,64]{1,0:T(8,128)} %copy.65) | copy-start | bytes 393220
  62.5 4.9 %copy-start.17 = (f32[512,64]{1,0:T(8,128)S(1)}, f32[512,64]{1,0:T(8,128)}, u32[]{:S(2)}) copy-start(f32[512,64]{1,0:T(8,128)} %copy.67) | copy-start | bytes 393220
  65.3 74.0 %collective-permute-start.3 = (f32[132096]{0:T(1024)}, f32[132096]{0:T(1024)}, u32[]{:S(2)}, u32[]{:S(2)}) collective-permute-start(f32[132096]{0:T(1024)} %fusion.107), channel_id=1, source_target_pairs={{0,16},{8,24},{16,32},{24,40},{32,48},{40,56},{1,17},{9,25},{17,33... | collective-permute-start | bytes 1585160 | tf_op jit(solution)/shard_map/ppermute | solution.py:16
  73.0 7.1 %copy-start.7 = (pred[512,576]{0,1:T(8,128)(4,1)S(1)}, pred[512,576]{0,1:T(8,128)(4,1)}, u32[]{:S(2)}) copy-start(pred[512,576]{0,1:T(8,128)(4,1)} %get-tuple-element.29) | copy-start | bytes 884740
  76.5 3.7 %copy-start.2 = (f32[576,512,8]{1,0,2:T(8,128)}, f32[576,512,8]{1,0,2:T(8,128)S(1)}, u32[]{:S(2)}) copy-start(f32[576,512,8]{1,0,2:T(8,128)S(1)} %get-tuple-element.35) | copy-start | bytes 28311556
  121.6 10.5 %copy-start.8 = (pred[512,576]{0,1:T(8,128)(4,1)S(1)}, pred[512,576]{0,1:T(8,128)(4,1)}, u32[]{:S(2)}) copy-start(pred[512,576]{0,1:T(8,128)(4,1)} %get-tuple-element.29) | copy-start | bytes 884740
  121.6 10.5 %copy-start.23 = (bf16[512,128]{1,0:T(8,128)(2,1)S(1)}, bf16[512,128]{1,0:T(8,128)(2,1)}, u32[]{:S(2)}) copy-start(bf16[512,128]{1,0:T(8,128)(2,1)} %param.12) | copy-start | bytes 393220
  128.7 14.8 %collective-permute-start.5 = (f32[132096]{0:T(1024)S(1)}, f32[132096]{0:T(1024)S(1)}, u32[]{:S(2)}, u32[]{:S(2)}) collective-permute-start(f32[132096]{0:T(1024)S(1)} %reduce_sum.87), channel_id=1, source_target_pairs={{0,64},{64,128},{128,192},{1,65},{65,129},{129,193},{2,66},{66,130... | collective-permute-start | bytes 1585160 | tf_op jit(solution)/shard_map/ppermute | solution.py:16
  139.3 10.2 %copy-start.15 = (f32[512,8,64]{0,2,1:T(8,128)S(1)}, f32[512,8,64]{0,2,1:T(8,128)}, u32[]{:S(2)}) copy-start(f32[512,8,64]{0,2,1:T(8,128)} %get-tuple-element.31) | copy-start | bytes 3145732
  140.6 9.2 %copy-start.14 = (bf16[576,8,128]{2,1,0:T(8,128)(2,1)S(1)}, bf16[576,8,128]{2,1,0:T(8,128)(2,1)}, u32[]{:S(2)}) copy-start(bf16[576,8,128]{2,1,0:T(8,128)(2,1)} %fusion.14) | copy-start | bytes 3538948
  140.6 9.2 %copy-start.18 = (pred[512,576]{0,1:T(8,128)(4,1)S(1)}, pred[512,576]{0,1:T(8,128)(4,1)}, u32[]{:S(2)}) copy-start(pred[512,576]{0,1:T(8,128)(4,1)} %get-tuple-element.28) | copy-start | bytes 884740
  140.7 29.0 %collective-permute-start.4 = (f32[132096]{0:T(1024)S(1)}, f32[132096]{0:T(1024)S(1)}, u32[]{:S(2)}, u32[]{:S(2)}) collective-permute-start(f32[132096]{0:T(1024)S(1)} %add.177), channel_id=1, source_target_pairs={{0,32},{8,40},{16,48},{24,56},{1,33},{9,41},{17,49},{25,57},{2,34}... | collective-permute-start | bytes 1585160 | tf_op jit(solution)/shard_map/ppermute | solution.py:16
  143.5 26.2 %collective-permute-start.6 = (f32[132096]{0:T(1024)S(1)}, f32[132096]{0:T(1024)S(1)}, u32[]{:S(2)}, u32[]{:S(2)}) collective-permute-start(f32[132096]{0:T(1024)S(1)} %add.179), channel_id=1, source_target_pairs={{0,128},{64,192},{1,129},{65,193},{2,130},{66,194},{3,131},{67,195... | collective-permute-start | bytes 1585160 | tf_op jit(solution)/shard_map/ppermute | solution.py:16
  149.8 19.9 %copy-start.11 = (f32[132096]{0:T(1024)S(1)}, f32[132096]{0:T(1024)}, u32[]{:S(2)}) copy-start(f32[132096]{0:T(1024)} %copy-done.9) | copy-start | bytes 1585156
  171.2 2.3 %copy-start.29 = (bf16[8,512,576]{1,2,0:T(8,128)(2,1)S(1)}, bf16[8,512,576]{1,2,0:T(8,128)(2,1)}, u32[]{:S(2)}) copy-start(bf16[8,512,576]{1,2,0:T(8,128)(2,1)} %get-tuple-element.37) | copy-start | bytes 14155780
  172.0 2.5 %copy-start.28 = (f32[128,8,512]{2,0,1:T(8,128)S(1)}, f32[128,8,512]{2,0,1:T(8,128)}, u32[]{:S(2)}) copy-start(f32[128,8,512]{2,0,1:T(8,128)} %fusion.10) | copy-start | bytes 6291460
  176.7 21.8 %copy-start.1 = (bf16[8,128,64]{1,2,0:T(8,128)(2,1)S(1)}, bf16[8,128,64]{1,2,0:T(8,128)(2,1)}, u32[]{:S(2)}) copy-start(bf16[8,128,64]{1,2,0:T(8,128)(2,1)} %param.14) | copy-start | bytes 393220
  (7 other events, 12.7 us)
Sparse Core Ops, SparseCore 0:
  36.5 80.2 all-gather.2
